TPU v7x, 512 devices: a whole 4x4x16 slice. The times are simulated.
512 devices in a mesh: cuts: 16 (over z_lo, core), stem: 32 (over z_hi, x, y).
Axes of the slice: x: 4, y: 4, z: 16 (z_hi: 2, z_lo: 8; z = z_hi * 8 + z_lo), core: 2. Of those that a mesh axis runs over, the one named last changes fastest.
Arguments:
- stem_tensor: bfloat16 [32, 16384, 2, 512], P('cuts', 'stem'), may hold values from -6 to 6
- branch_tensor: bfloat16 [32, 512, 2, 512], P('cuts', 'stem'), may hold values from -0.1875 to 0.1875
- open_tensor: bfloat16 [32, 16384, 2, 512], P('cuts', 'stem'), may hold values from -0.75 to 0.75
- open_order: int32 [32, 512], P('cuts'), may hold values from 0 to 511, each once within a row
Outputs:
- amplitudes: float32 [32, 512, 2, 512], P('stem', 'cuts')
Inputs may be any that keep to these rules, and one draw needn't show every extreme that they name: Each row of open_order holds every number of 0 to 511 once.
All inputs are finite; a program needn't handle non-finite values.
Results may differ from a plain program's by a relative error of at most 0.0003.
Values may be sent and summed in bfloat16 or wider, within the bound.
No kernel may reach another device: no remote copies, remote signals or barrier semaphores. Data moves between devices by JAX's collectives and lax.ppermute only.
A program may use at most 64 MiB of HBM per device.

v0:
```python
from functools import partial
import jax
import jax.numpy as jnp
from jax import lax
from jax.sharding import PartitionSpec as P


def from_behind(value, axis, steps):
    count = lax.axis_size(axis)
    pairs = [(source, (source + steps) % count) for source in range(count)]
    return lax.ppermute(value, axis, pairs)


def expand_branch(segment):
    top_rows = jnp.concatenate([segment[..., 0, :], segment[..., 1, :]], axis=-1)
    bottom_rows = jnp.concatenate([-segment[..., 1, :], segment[..., 0, :]], axis=-1)
    return jnp.concatenate([top_rows, bottom_rows], axis=-2)


def fold_rows(stem_block, running, segment, offset):
    stem_cols = stem_block
    stem_cols = stem_cols.reshape(stem_cols.shape[0], -1)
    product = jnp.dot(stem_cols, expand_branch(segment), preferred_element_type=jnp.float32)
    return product.reshape(running.shape)


def body(stem_tensor, branch_tensor, open_tensor, open_order):
    slice_count = stem_tensor.shape[0]
    row_count = stem_tensor.shape[1]
    width = stem_tensor.shape[3]
    image_list = []
    for slice_pos in range(slice_count):
        initial = jnp.zeros((row_count, 2, width), jnp.float32)
        folder = partial(fold_rows, stem_tensor[slice_pos])
        image_list.append(
            folder(
                initial,
                lax.all_gather(branch_tensor[slice_pos], "stem", axis=0, tiled=True),
                jnp.int32(0),
            )
        )
    local_sum = jnp.zeros((row_count, 2, width), jnp.float32)
    for slice_pos in range(slice_count):
        placed = jnp.take(image_list[slice_pos], open_order[slice_pos], axis=2)
        opened = open_tensor[slice_pos].astype(jnp.float32)
        real_part = placed[:, 0, :] * opened[:, 0, :] - placed[:, 1, :] * opened[:, 1, :]
        imag_part = placed[:, 0, :] * opened[:, 1, :] + placed[:, 1, :] * opened[:, 0, :]
        local_sum = local_sum + jnp.stack([real_part, imag_part], axis=1)
    cut_count = lax.axis_size("cuts")
    block_rows = row_count // cut_count
    cut_index = lax.axis_index("cuts")

    def pick_block(turn):
        start_row = (cut_index + cut_count - 1 - turn) % cut_count * block_rows
        return lax.dynamic_slice_in_dim(local_sum, start_row, block_rows, 0)

    def pass_along(turn, running):
        return from_behind(running, "cuts", 1) + pick_block(turn)

    running = lax.fori_loop(1, cut_count, pass_along, pick_block(0))
    return running.reshape(1, block_rows, 2, width)


def solution(mesh):
    return jax.shard_map(
        body,
        mesh=mesh,
        in_specs=(
            P("cuts", "stem", None, None),
            P("cuts", "stem", None, None),
            P("cuts", "stem", None, None),
            P("cuts", None),
        ),
        out_specs=P("stem", "cuts", None, None),
        check_vma=False,
    )
```

profile of v0, /device:TPU:2, one launch (start us, length us, event | category | flops | bytes accessed | tf_op | source)
XLA Modules:
  0.0 490.7 jit_solution(4633315407787686485)
XLA Ops:
  24.9 103.1 %all-gather.7.cloned.1.call-done = bf16[1,512,2,512]{3,1,2,0:T(8,128)(2,1)} async-done(((bf16[1,16,2,512]{3,1,2,0:T(8,128)(2,1)}), bf16[1,512,2,512]{3,1,2,0:T(8,128)(2,1)}) %all-gather.7.cloned.1.call-update) | async-done | bytes 1048592 | tf_op jit(solution)/shard_map/all_gather | solution.py:38
  130.4 104.0 %all-gather.5.cloned.1.call-done = bf16[1,512,2,512]{3,1,2,0:T(8,128)(2,1)} async-done(((bf16[1,16,2,512]{3,1,2,0:T(8,128)(2,1)}), bf16[1,512,2,512]{3,1,2,0:T(8,128)(2,1)}) %all-gather.5.cloned.1.call-update) | async-done | bytes 1048592 | tf_op jit(solution)/shard_map/all_gather | solution.py:38
  243.2 4.4 gather_fusion.1
  247.6 4.2 select_bitcast_fusion
  251.7 4.3 gather_fusion
  259.2 7.4 %multiply_subtract_fusion = (f32[512,1,512]{0,1,2:T(1,128)S(1)}, f32[512,1,512]{0,1,2:T(1,128)S(1)}, f32[512,1,512]{0,1,2:T(1,128)S(1)}, f32[512,1,512]{0,1,2:T(1,128)S(1)}) fusion(f32[512,2,512]{0,1,2:T(2,128)S(1)} %copy-done.1, f32[512,2,512]{0,1,2:T(2,128)} %select_bitcast_fusion, f32[512,2,512]{0,1,2:T(2,128)S(1)} %copy-done.2, ...), kind=kLoop, calls=%fused_computation.25 | loop fusion | flops 3145728 | bytes 12582912 | tf_op jit(solution)/shard_map/sub | solution.py:46
  266.7 3.5 maximum_add_fusion
  270.1 4.1 copy.14
  275.0 208.2 %while.15 = (s32[]{:T(128)}, f32[32,2,512]{2,1,0:T(2,128)S(1)}, s32[]{:T(128)}, f32[512,2,512]{2,1,0:T(2,128)}, s32[]{:T(128)}, /*index=5*/s32[]{:T(128)}, s32[]{:T(128)}, s32[]{:T(128)}, s32[]{:T(128)}, s32[]{:T(128)}) while((s32[]{:T(128)}, f32[32,2,512]{2,1,0:T(2,128)S(1)}, s32[]{:T(128)}, f32[512,2,512]{2,1,0:T(2,128)}, s32[]{:T(128)}, ...), condition=%wide.region_1.3_spmd, body=%wide.region_0.0_spmd.sunk | while | flops 32786 | bytes 917816 | solution.py:60
  277.0 10.9 %collective-permute-done = f32[32,2,512]{2,1,0:T(2,128)S(1)} collective-permute-done((f32[32,2,512]{2,1,0:T(2,128)S(1)}, f32[32,2,512]{2,1,0:T(2,128)S(1)}, u32[]{:S(2)}, u32[]{:S(2)}) %collective-permute-start) | collective-permute-done | bytes 131104 | tf_op jit(solution)/shard_map/while/body/eval_jaxpr/ppermute | solution.py:11
  290.9 10.9 %collective-permute-done = f32[32,2,512]{2,1,0:T(2,128)S(1)} collective-permute-done((f32[32,2,512]{2,1,0:T(2,128)S(1)}, f32[32,2,512]{2,1,0:T(2,128)S(1)}, u32[]{:S(2)}, u32[]{:S(2)}) %collective-permute-start) | collective-permute-done | bytes 131104 | tf_op jit(solution)/shard_map/while/body/eval_jaxpr/ppermute | solution.py:11
  304.8 10.9 %collective-permute-done = f32[32,2,512]{2,1,0:T(2,128)S(1)} collective-permute-done((f32[32,2,512]{2,1,0:T(2,128)S(1)}, f32[32,2,512]{2,1,0:T(2,128)S(1)}, u32[]{:S(2)}, u32[]{:S(2)}) %collective-permute-start) | collective-permute-done | bytes 131104 | tf_op jit(solution)/shard_map/while/body/eval_jaxpr/ppermute | solution.py:11
  318.6 10.9 %collective-permute-done = f32[32,2,512]{2,1,0:T(2,128)S(1)} collective-permute-done((f32[32,2,512]{2,1,0:T(2,128)S(1)}, f32[32,2,512]{2,1,0:T(2,128)S(1)}, u32[]{:S(2)}, u32[]{:S(2)}) %collective-permute-start) | collective-permute-done | bytes 131104 | tf_op jit(solution)/shard_map/while/body/eval_jaxpr/ppermute | solution.py:11
  332.5 10.9 %collective-permute-done = f32[32,2,512]{2,1,0:T(2,128)S(1)} collective-permute-done((f32[32,2,512]{2,1,0:T(2,128)S(1)}, f32[32,2,512]{2,1,0:T(2,128)S(1)}, u32[]{:S(2)}, u32[]{:S(2)}) %collective-permute-start) | collective-permute-done | bytes 131104 | tf_op jit(solution)/shard_map/while/body/eval_jaxpr/ppermute | solution.py:11
  346.4 10.9 %collective-permute-done = f32[32,2,512]{2,1,0:T(2,128)S(1)} collective-permute-done((f32[32,2,512]{2,1,0:T(2,128)S(1)}, f32[32,2,512]{2,1,0:T(2,128)S(1)}, u32[]{:S(2)}, u32[]{:S(2)}) %collective-permute-start) | collective-permute-done | bytes 131104 | tf_op jit(solution)/shard_map/while/body/eval_jaxpr/ppermute | solution.py:11
  360.3 10.9 %collective-permute-done = f32[32,2,512]{2,1,0:T(2,128)S(1)} collective-permute-done((f32[32,2,512]{2,1,0:T(2,128)S(1)}, f32[32,2,512]{2,1,0:T(2,128)S(1)}, u32[]{:S(2)}, u32[]{:S(2)}) %collective-permute-start) | collective-permute-done | bytes 131104 | tf_op jit(solution)/shard_map/while/body/eval_jaxpr/ppermute | solution.py:11
  374.2 10.9 %collective-permute-done = f32[32,2,512]{2,1,0:T(2,128)S(1)} collective-permute-done((f32[32,2,512]{2,1,0:T(2,128)S(1)}, f32[32,2,512]{2,1,0:T(2,128)S(1)}, u32[]{:S(2)}, u32[]{:S(2)}) %collective-permute-start) | collective-permute-done | bytes 131104 | tf_op jit(solution)/shard_map/while/body/eval_jaxpr/ppermute | solution.py:11
  388.0 10.9 %collective-permute-done = f32[32,2,512]{2,1,0:T(2,128)S(1)} collective-permute-done((f32[32,2,512]{2,1,0:T(2,128)S(1)}, f32[32,2,512]{2,1,0:T(2,128)S(1)}, u32[]{:S(2)}, u32[]{:S(2)}) %collective-permute-start) | collective-permute-done | bytes 131104 | tf_op jit(solution)/shard_map/while/body/eval_jaxpr/ppermute | solution.py:11
  401.9 10.9 %collective-permute-done = f32[32,2,512]{2,1,0:T(2,128)S(1)} collective-permute-done((f32[32,2,512]{2,1,0:T(2,128)S(1)}, f32[32,2,512]{2,1,0:T(2,128)S(1)}, u32[]{:S(2)}, u32[]{:S(2)}) %collective-permute-start) | collective-permute-done | bytes 131104 | tf_op jit(solution)/shard_map/while/body/eval_jaxpr/ppermute | solution.py:11
  415.8 10.9 %collective-permute-done = f32[32,2,512]{2,1,0:T(2,128)S(1)} collective-permute-done((f32[32,2,512]{2,1,0:T(2,128)S(1)}, f32[32,2,512]{2,1,0:T(2,128)S(1)}, u32[]{:S(2)}, u32[]{:S(2)}) %collective-permute-start) | collective-permute-done | bytes 131104 | tf_op jit(solution)/shard_map/while/body/eval_jaxpr/ppermute | solution.py:11
  429.7 10.9 %collective-permute-done = f32[32,2,512]{2,1,0:T(2,128)S(1)} collective-permute-done((f32[32,2,512]{2,1,0:T(2,128)S(1)}, f32[32,2,512]{2,1,0:T(2,128)S(1)}, u32[]{:S(2)}, u32[]{:S(2)}) %collective-permute-start) | collective-permute-done | bytes 131104 | tf_op jit(solution)/shard_map/while/body/eval_jaxpr/ppermute | solution.py:11
  443.5 10.9 %collective-permute-done = f32[32,2,512]{2,1,0:T(2,128)S(1)} collective-permute-done((f32[32,2,512]{2,1,0:T(2,128)S(1)}, f32[32,2,512]{2,1,0:T(2,128)S(1)}, u32[]{:S(2)}, u32[]{:S(2)}) %collective-permute-start) | collective-permute-done | bytes 131104 | tf_op jit(solution)/shard_map/while/body/eval_jaxpr/ppermute | solution.py:11
  457.4 10.9 %collective-permute-done = f32[32,2,512]{2,1,0:T(2,128)S(1)} collective-permute-done((f32[32,2,512]{2,1,0:T(2,128)S(1)}, f32[32,2,512]{2,1,0:T(2,128)S(1)}, u32[]{:S(2)}, u32[]{:S(2)}) %collective-permute-start) | collective-permute-done | bytes 131104 | tf_op jit(solution)/shard_map/while/body/eval_jaxpr/ppermute | solution.py:11
  471.3 10.9 %collective-permute-done = f32[32,2,512]{2,1,0:T(2,128)S(1)} collective-permute-done((f32[32,2,512]{2,1,0:T(2,128)S(1)}, f32[32,2,512]{2,1,0:T(2,128)S(1)}, u32[]{:S(2)}, u32[]{:S(2)}) %collective-permute-start) | collective-permute-done | bytes 131104 | tf_op jit(solution)/shard_map/while/body/eval_jaxpr/ppermute | solution.py:11
  (83 shorter events, 77.3 us)
Async XLA Ops:
  6.5 121.5 %all-gather.7.cloned.1.call-start = ((), (), s32[]{:S(2)}) async-start(), calls=%async_computation.1 | async-start | bytes 1081344 | tf_op jit(solution)/shard_map/all_gather | solution.py:38
  8.0 226.4 %all-gather.5.cloned.1.call-start = ((), (), s32[]{:S(2)}) async-start(), calls=%async_computation | async-start | bytes 1081344 | tf_op jit(solution)/shard_map/all_gather | solution.py:38
  8.8 2.9 copy-start.9
  8.8 2.9 copy-start.5
  130.4 105.6 %copy-start.7 = (bf16[64,8,2,512]{3,1,2,0:T(8,128)(2,1)S(1)}, bf16[64,8,2,512]{3,1,2,0:T(8,128)(2,1)}, u32[]{:S(2)}) copy-start(bf16[64,8,2,512]{3,1,2,0:T(8,128)(2,1)} %copy.20) | copy-start | bytes 3145732
  237.3 1.6 copy-start.6
  247.6 4.2 copy-start
  256.1 3.2 copy-start.1
  256.1 3.2 copy-start.2
  275.1 12.9 %collective-permute-start = (f32[32,2,512]{2,1,0:T(2,128)S(1)}, f32[32,2,512]{2,1,0:T(2,128)S(1)}, u32[]{:S(2)}, u32[]{:S(2)}) collective-permute-start(f32[32,2,512]{2,1,0:T(2,128)S(1)} %get-tuple-element.188), channel_id=1, source_target_pairs={{0,32},{32,64},{64,96},{96,128},{128,160},{160,192},{192,224},{224... | collective-permute-start | bytes 393224 | tf_op jit(solution)/shard_map/while/body/eval_jaxpr/ppermute | solution.py:11
  288.9 12.9 %collective-permute-start = (f32[32,2,512]{2,1,0:T(2,128)S(1)}, f32[32,2,512]{2,1,0:T(2,128)S(1)}, u32[]{:S(2)}, u32[]{:S(2)}) collective-permute-start(f32[32,2,512]{2,1,0:T(2,128)S(1)} %get-tuple-element.188), channel_id=1, source_target_pairs={{0,32},{32,64},{64,96},{96,128},{128,160},{160,192},{192,224},{224... | collective-permute-start | bytes 393224 | tf_op jit(solution)/shard_map/while/body/eval_jaxpr/ppermute | solution.py:11
  302.8 12.9 %collective-permute-start = (f32[32,2,512]{2,1,0:T(2,128)S(1)}, f32[32,2,512]{2,1,0:T(2,128)S(1)}, u32[]{:S(2)}, u32[]{:S(2)}) collective-permute-start(f32[32,2,512]{2,1,0:T(2,128)S(1)} %get-tuple-element.188), channel_id=1, source_target_pairs={{0,32},{32,64},{64,96},{96,128},{128,160},{160,192},{192,224},{224... | collective-permute-start | bytes 393224 | tf_op jit(solution)/shard_map/while/body/eval_jaxpr/ppermute | solution.py:11
  316.7 12.9 %collective-permute-start = (f32[32,2,512]{2,1,0:T(2,128)S(1)}, f32[32,2,512]{2,1,0:T(2,128)S(1)}, u32[]{:S(2)}, u32[]{:S(2)}) collective-permute-start(f32[32,2,512]{2,1,0:T(2,128)S(1)} %get-tuple-element.188), channel_id=1, source_target_pairs={{0,32},{32,64},{64,96},{96,128},{128,160},{160,192},{192,224},{224... | collective-permute-start | bytes 393224 | tf_op jit(solution)/shard_map/while/body/eval_jaxpr/ppermute | solution.py:11
  330.6 12.9 %collective-permute-start = (f32[32,2,512]{2,1,0:T(2,128)S(1)}, f32[32,2,512]{2,1,0:T(2,128)S(1)}, u32[]{:S(2)}, u32[]{:S(2)}) collective-permute-start(f32[32,2,512]{2,1,0:T(2,128)S(1)} %get-tuple-element.188), channel_id=1, source_target_pairs={{0,32},{32,64},{64,96},{96,128},{128,160},{160,192},{192,224},{224... | collective-permute-start | bytes 393224 | tf_op jit(solution)/shard_map/while/body/eval_jaxpr/ppermute | solution.py:11
  344.4 12.9 %collective-permute-start = (f32[32,2,512]{2,1,0:T(2,128)S(1)}, f32[32,2,512]{2,1,0:T(2,128)S(1)}, u32[]{:S(2)}, u32[]{:S(2)}) collective-permute-start(f32[32,2,512]{2,1,0:T(2,128)S(1)} %get-tuple-element.188), channel_id=1, source_target_pairs={{0,32},{32,64},{64,96},{96,128},{128,160},{160,192},{192,224},{224... | collective-permute-start | bytes 393224 | tf_op jit(solution)/shard_map/while/body/eval_jaxpr/ppermute | solution.py:11
  358.3 12.9 %collective-permute-start = (f32[32,2,512]{2,1,0:T(2,128)S(1)}, f32[32,2,512]{2,1,0:T(2,128)S(1)}, u32[]{:S(2)}, u32[]{:S(2)}) collective-permute-start(f32[32,2,512]{2,1,0:T(2,128)S(1)} %get-tuple-element.188), channel_id=1, source_target_pairs={{0,32},{32,64},{64,96},{96,128},{128,160},{160,192},{192,224},{224... | collective-permute-start | bytes 393224 | tf_op jit(solution)/shard_map/while/body/eval_jaxpr/ppermute | solution.py:11
  372.2 12.9 %collective-permute-start = (f32[32,2,512]{2,1,0:T(2,128)S(1)}, f32[32,2,512]{2,1,0:T(2,128)S(1)}, u32[]{:S(2)}, u32[]{:S(2)}) collective-permute-start(f32[32,2,512]{2,1,0:T(2,128)S(1)} %get-tuple-element.188), channel_id=1, source_target_pairs={{0,32},{32,64},{64,96},{96,128},{128,160},{160,192},{192,224},{224... | collective-permute-start | bytes 393224 | tf_op jit(solution)/shard_map/while/body/eval_jaxpr/ppermute | solution.py:11
  386.1 12.9 %collective-permute-start = (f32[32,2,512]{2,1,0:T(2,128)S(1)}, f32[32,2,512]{2,1,0:T(2,128)S(1)}, u32[]{:S(2)}, u32[]{:S(2)}) collective-permute-start(f32[32,2,512]{2,1,0:T(2,128)S(1)} %get-tuple-element.188), channel_id=1, source_target_pairs={{0,32},{32,64},{64,96},{96,128},{128,160},{160,192},{192,224},{224... | collective-permute-start | bytes 393224 | tf_op jit(solution)/shard_map/while/body/eval_jaxpr/ppermute | solution.py:11
  400.0 12.9 %collective-permute-start = (f32[32,2,512]{2,1,0:T(2,128)S(1)}, f32[32,2,512]{2,1,0:T(2,128)S(1)}, u32[]{:S(2)}, u32[]{:S(2)}) collective-permute-start(f32[32,2,512]{2,1,0:T(2,128)S(1)} %get-tuple-element.188), channel_id=1, source_target_pairs={{0,32},{32,64},{64,96},{96,128},{128,160},{160,192},{192,224},{224... | collective-permute-start | bytes 393224 | tf_op jit(solution)/shard_map/while/body/eval_jaxpr/ppermute | solution.py:11
  413.8 12.9 %collective-permute-start = (f32[32,2,512]{2,1,0:T(2,128)S(1)}, f32[32,2,512]{2,1,0:T(2,128)S(1)}, u32[]{:S(2)}, u32[]{:S(2)}) collective-permute-start(f32[32,2,512]{2,1,0:T(2,128)S(1)} %get-tuple-element.188), channel_id=1, source_target_pairs={{0,32},{32,64},{64,96},{96,128},{128,160},{160,192},{192,224},{224... | collective-permute-start | bytes 393224 | tf_op jit(solution)/shard_map/while/body/eval_jaxpr/ppermute | solution.py:11
  427.7 12.9 %collective-permute-start = (f32[32,2,512]{2,1,0:T(2,128)S(1)}, f32[32,2,512]{2,1,0:T(2,128)S(1)}, u32[]{:S(2)}, u32[]{:S(2)}) collective-permute-start(f32[32,2,512]{2,1,0:T(2,128)S(1)} %get-tuple-element.188), channel_id=1, source_target_pairs={{0,32},{32,64},{64,96},{96,128},{128,160},{160,192},{192,224},{224... | collective-permute-start | bytes 393224 | tf_op jit(solution)/shard_map/while/body/eval_jaxpr/ppermute | solution.py:11
  441.6 12.9 %collective-permute-start = (f32[32,2,512]{2,1,0:T(2,128)S(1)}, f32[32,2,512]{2,1,0:T(2,128)S(1)}, u32[]{:S(2)}, u32[]{:S(2)}) collective-permute-start(f32[32,2,512]{2,1,0:T(2,128)S(1)} %get-tuple-element.188), channel_id=1, source_target_pairs={{0,32},{32,64},{64,96},{96,128},{128,160},{160,192},{192,224},{224... | collective-permute-start | bytes 393224 | tf_op jit(solution)/shard_map/while/body/eval_jaxpr/ppermute | solution.py:11
  455.5 12.9 %collective-permute-start = (f32[32,2,512]{2,1,0:T(2,128)S(1)}, f32[32,2,512]{2,1,0:T(2,128)S(1)}, u32[]{:S(2)}, u32[]{:S(2)}) collective-permute-start(f32[32,2,512]{2,1,0:T(2,128)S(1)} %get-tuple-element.188), channel_id=1, source_target_pairs={{0,32},{32,64},{64,96},{96,128},{128,160},{160,192},{192,224},{224... | collective-permute-start | bytes 393224 | tf_op jit(solution)/shard_map/while/body/eval_jaxpr/ppermute | solution.py:11
  469.3 12.9 %collective-permute-start = (f32[32,2,512]{2,1,0:T(2,128)S(1)}, f32[32,2,512]{2,1,0:T(2,128)S(1)}, u32[]{:S(2)}, u32[]{:S(2)}) collective-permute-start(f32[32,2,512]{2,1,0:T(2,128)S(1)} %get-tuple-element.188), channel_id=1, source_target_pairs={{0,32},{32,64},{64,96},{96,128},{128,160},{160,192},{192,224},{224... | collective-permute-start | bytes 393224 | tf_op jit(solution)/shard_map/while/body/eval_jaxpr/ppermute | solution.py:11
  (3 other events, 3.5 us)
Sparse Core Ops, SparseCore 0:
  11.8 116.2 all-gather.6
  132.5 101.9 all-gather.4
where the time goes:
time: 492 us; the launch traced here: 491 us
  waiting for transfers between devices  371 us (75%)
  other arithmetic  38 us (8%)
  local copies, waits for them, and re-layouts  35.6 us (7%)
  starting transfers between devices  28.9 us (6%)
  between operations  13.7 us (3%)
    all_gather x2, waiting for transfers between devices, body(): lax.all_gather(branch_tensor[slice_pos], 'stem', axis=0, tiled=True)  207 us
    ppermute x15, waiting for transfers between devices, from_behind(): return lax.ppermute(value, axis, pairs)  164 us
    ppermute x15, starting transfers between devices, from_behind(): return lax.ppermute(value, axis, pairs)  28.8 us
    add x15, other arithmetic, pass_along(): return from_behind(running, 'cuts', 1) + pick_block(turn)  14.6 us
  transfers between devices with their start and end apart: 17, of which 17 were waited for; matrix products, arithmetic and copies ran while one was open for 4% of the time, Pallas kernels for 0%

commit v1 on v0

--- a/solution.py
+++ b/solution.py
@@ -35,7 +35,12 @@
         image_list.append(
             folder(
                 initial,
-                lax.all_gather(branch_tensor[slice_pos], "stem", axis=0, tiled=True),
+                jnp.concatenate(
+                    lax.all_to_all(
+                        jnp.stack([branch_tensor[slice_pos]] * lax.axis_size("stem")), "stem", 0, 0
+                    ),
+                    axis=0,
+                ),
                 jnp.int32(0),
             )
         )

time: 492 us -> 359 us (0.73)
  the two profiles are of different devices: /device:TPU:2 before, /device:TPU:8 now
where the time goes in v1:
time: 359 us; the launch traced here: 358 us
  waiting for transfers between devices  193 us (54%)
  starting transfers between devices  87.7 us (24%)
  local copies, waits for them, and re-layouts  37.5 us (10%)
  other arithmetic  36.8 us (10%)
    ppermute x15, waiting for transfers between devices, from_behind(): return lax.ppermute(value, axis, pairs)  151 us
    ppermute x15, starting transfers between devices, from_behind(): return lax.ppermute(value, axis, pairs)  61.7 us
    all_to_all x2, waiting for transfers between devices, body(): lax.all_to_all(jnp.stack([branch_tensor[slice_pos]] * lax.axis_size('stem...  41.9 us
    all_to_all x2, starting transfers between devices, body(): lax.all_to_all(jnp.stack([branch_tensor[slice_pos]] * lax.axis_size('stem...  25.9 us
    add x15, other arithmetic, pass_along(): return from_behind(running, 'cuts', 1) + pick_block(turn)  14.6 us
    unnamed x22, local copies, waits for them, and re-layouts  11.1 us
    gather x2, local copies, waits for them, and re-layouts, body(): placed = jnp.take(image_list[slice_pos], open_order[slice_pos], axis=2)  8.68 us
    select_n x4, other arithmetic, body(): placed = jnp.take(image_list[slice_pos], open_order[slice_pos], axis=2)  7.35 us
  transfers between devices with their start and end apart: 17, of which 17 were waited for; matrix products, arithmetic and copies ran while one was open for 5% of the time, Pallas kernels for 0%

profile of v1, /device:TPU:8, one launch (start us, length us, event | category | flops | bytes accessed | tf_op | source)
XLA Modules:
  0.0 358.2 jit_solution(11829776152661926602)
XLA Ops:
  2.0 20.8 %all-to-all-start = ((bf16[32,16,2,512]{3,1,2,0:T(8,128)(2,1)}), bf16[32,16,2,512]{3,1,2,0:T(8,128)(2,1)S(1)}, u32[]{:S(2)}, u32[]{:S(2)}) async-start(bf16[32,16,2,512]{3,1,2,0:T(8,128)(2,1)} %stack.16), calls=%async_computation | async-start | bytes 2097152 | tf_op jit(solution)/shard_map/all_to_all | solution.py:39
  22.8 29.7 %all-to-all-done = bf16[32,16,2,512]{3,1,2,0:T(8,128)(2,1)S(1)} async-done(((bf16[32,16,2,512]{3,1,2,0:T(8,128)(2,1)}), bf16[32,16,2,512]{3,1,2,0:T(8,128)(2,1)S(1)}, u32[]{:S(2)}, u32[]{:S(2)}) %all-to-all-start) | async-done | bytes 1048608 | tf_op jit(solution)/shard_map/all_to_all | solution.py:39
  53.6 5.1 %all-to-all-start.1 = ((bf16[32,16,2,512]{3,1,2,0:T(8,128)(2,1)}), bf16[32,16,2,512]{3,1,2,0:T(8,128)(2,1)}, u32[]{:S(2)}, u32[]{:S(2)}) async-start(bf16[32,16,2,512]{3,1,2,0:T(8,128)(2,1)} %stack.18), calls=%async_computation.1 | async-start | bytes 2097152 | tf_op jit(solution)/shard_map/all_to_all | solution.py:39
  67.1 4.7 %copy.25 = bf16[1,512,2,512]{1,2,3,0:T(2,128)(2,1)S(1)} copy(bf16[1,512,2,512]{3,2,1,0:T(2,128)(2,1)} %get-tuple-element.145) | data formatting | bytes 2097152
  76.2 12.2 %all-to-all-done.1 = bf16[32,16,2,512]{3,1,2,0:T(8,128)(2,1)} async-done(((bf16[32,16,2,512]{3,1,2,0:T(8,128)(2,1)}), bf16[32,16,2,512]{3,1,2,0:T(8,128)(2,1)}, u32[]{:S(2)}, u32[]{:S(2)}) %all-to-all-start.1) | async-done | bytes 1048608 | tf_op jit(solution)/shard_map/all_to_all | solution.py:39
  98.2 4.4 %gather_fusion = f32[512,512,2]{1,2,0:T(2,128)} fusion(f32[512,2,512]{0,1,2:T(2,128)S(1)} %copy.17, s32[1024]{0:T(1024)S(1)} %pad_clamp_fusion.1), kind=kCustom, calls=%fused_computation.clone | custom fusion | bytes 4196352 | tf_op jit(solution)/shard_map/jit(_take)/gather | solution.py:49
  114.2 7.2 %multiply_subtract_fusion = (f32[512,1,512]{0,1,2:T(1,128)S(1)}, f32[512,1,512]{0,1,2:T(1,128)S(1)}, f32[512,1,512]{0,1,2:T(1,128)S(1)}, f32[512,1,512]{0,1,2:T(1,128)S(1)}) fusion(f32[512,2,512]{0,1,2:T(2,128)S(1)} %copy-done.1, f32[512,2,512]{0,1,2:T(2,128)S(1)} %select_bitcast_fusion, f32[512,2,512]{0,1,2:T(2,128)S(1)} %copy-done.2, ...), kind=kLoop, calls=%fused_computation.25 | loop fusion | flops 3145728 | bytes 12582912 | tf_op jit(solution)/shard_map/sub | solution.py:51
  129.8 227.7 %while.15 = (s32[]{:T(128)}, f32[32,2,512]{2,1,0:T(2,128)S(1)}, s32[]{:T(128)}, f32[512,2,512]{2,1,0:T(2,128)}, s32[]{:T(128)}, /*index=5*/s32[]{:T(128)}, s32[]{:T(128)}, s32[]{:T(128)}, s32[]{:T(128)}, s32[]{:T(128)}) while((s32[]{:T(128)}, f32[32,2,512]{2,1,0:T(2,128)S(1)}, s32[]{:T(128)}, f32[512,2,512]{2,1,0:T(2,128)}, s32[]{:T(128)}, ...), condition=%wide.region_1.3_spmd, body=%wide.region_0.0_spmd.sunk | while | flops 32786 | bytes 917816 | solution.py:65
  131.8 10.9 %collective-permute-done = f32[32,2,512]{2,1,0:T(2,128)S(1)} collective-permute-done((f32[32,2,512]{2,1,0:T(2,128)S(1)}, f32[32,2,512]{2,1,0:T(2,128)S(1)}, u32[]{:S(2)}, u32[]{:S(2)}) %collective-permute-start) | collective-permute-done | bytes 131104 | tf_op jit(solution)/shard_map/while/body/eval_jaxpr/ppermute | solution.py:11
  143.7 31.5 %collective-permute-start = (f32[32,2,512]{2,1,0:T(2,128)S(1)}, f32[32,2,512]{2,1,0:T(2,128)S(1)}, u32[]{:S(2)}, u32[]{:S(2)}) collective-permute-start(f32[32,2,512]{2,1,0:T(2,128)S(1)} %get-tuple-element.192), channel_id=1, source_target_pairs={{0,32},{32,64},{64,96},{96,128},{128,160},{160,192},{192,224},{224... | collective-permute-start | bytes 393224 | tf_op jit(solution)/shard_map/while/body/eval_jaxpr/ppermute | solution.py:11
  177.1 5.3 %collective-permute-start = (f32[32,2,512]{2,1,0:T(2,128)S(1)}, f32[32,2,512]{2,1,0:T(2,128)S(1)}, u32[]{:S(2)}, u32[]{:S(2)}) collective-permute-start(f32[32,2,512]{2,1,0:T(2,128)S(1)} %get-tuple-element.192), channel_id=1, source_target_pairs={{0,32},{32,64},{64,96},{96,128},{128,160},{160,192},{192,224},{224... | collective-permute-start | bytes 393224 | tf_op jit(solution)/shard_map/while/body/eval_jaxpr/ppermute | solution.py:11
  182.4 7.5 %collective-permute-done = f32[32,2,512]{2,1,0:T(2,128)S(1)} collective-permute-done((f32[32,2,512]{2,1,0:T(2,128)S(1)}, f32[32,2,512]{2,1,0:T(2,128)S(1)}, u32[]{:S(2)}, u32[]{:S(2)}) %collective-permute-start) | collective-permute-done | bytes 131104 | tf_op jit(solution)/shard_map/while/body/eval_jaxpr/ppermute | solution.py:11
  192.9 10.9 %collective-permute-done = f32[32,2,512]{2,1,0:T(2,128)S(1)} collective-permute-done((f32[32,2,512]{2,1,0:T(2,128)S(1)}, f32[32,2,512]{2,1,0:T(2,128)S(1)}, u32[]{:S(2)}, u32[]{:S(2)}) %collective-permute-start) | collective-permute-done | bytes 131104 | tf_op jit(solution)/shard_map/while/body/eval_jaxpr/ppermute | solution.py:11
  206.8 10.9 %collective-permute-done = f32[32,2,512]{2,1,0:T(2,128)S(1)} collective-permute-done((f32[32,2,512]{2,1,0:T(2,128)S(1)}, f32[32,2,512]{2,1,0:T(2,128)S(1)}, u32[]{:S(2)}, u32[]{:S(2)}) %collective-permute-start) | collective-permute-done | bytes 131104 | tf_op jit(solution)/shard_map/while/body/eval_jaxpr/ppermute | solution.py:11
  220.7 10.9 %collective-permute-done = f32[32,2,512]{2,1,0:T(2,128)S(1)} collective-permute-done((f32[32,2,512]{2,1,0:T(2,128)S(1)}, f32[32,2,512]{2,1,0:T(2,128)S(1)}, u32[]{:S(2)}, u32[]{:S(2)}) %collective-permute-start) | collective-permute-done | bytes 131104 | tf_op jit(solution)/shard_map/while/body/eval_jaxpr/ppermute | solution.py:11
  234.6 10.9 %collective-permute-done = f32[32,2,512]{2,1,0:T(2,128)S(1)} collective-permute-done((f32[32,2,512]{2,1,0:T(2,128)S(1)}, f32[32,2,512]{2,1,0:T(2,128)S(1)}, u32[]{:S(2)}, u32[]{:S(2)}) %collective-permute-start) | collective-permute-done | bytes 131104 | tf_op jit(solution)/shard_map/while/body/eval_jaxpr/ppermute | solution.py:11
  248.4 10.9 %collective-permute-done = f32[32,2,512]{2,1,0:T(2,128)S(1)} collective-permute-done((f32[32,2,512]{2,1,0:T(2,128)S(1)}, f32[32,2,512]{2,1,0:T(2,128)S(1)}, u32[]{:S(2)}, u32[]{:S(2)}) %collective-permute-start) | collective-permute-done | bytes 131104 | tf_op jit(solution)/shard_map/while/body/eval_jaxpr/ppermute | solution.py:11
  262.3 10.9 %collective-permute-done = f32[32,2,512]{2,1,0:T(2,128)S(1)} collective-permute-done((f32[32,2,512]{2,1,0:T(2,128)S(1)}, f32[32,2,512]{2,1,0:T(2,128)S(1)}, u32[]{:S(2)}, u32[]{:S(2)}) %collective-permute-start) | collective-permute-done | bytes 131104 | tf_op jit(solution)/shard_map/while/body/eval_jaxpr/ppermute | solution.py:11
  276.2 10.9 %collective-permute-done = f32[32,2,512]{2,1,0:T(2,128)S(1)} collective-permute-done((f32[32,2,512]{2,1,0:T(2,128)S(1)}, f32[32,2,512]{2,1,0:T(2,128)S(1)}, u32[]{:S(2)}, u32[]{:S(2)}) %collective-permute-start) | collective-permute-done | bytes 131104 | tf_op jit(solution)/shard_map/while/body/eval_jaxpr/ppermute | solution.py:11
  290.1 10.9 %collective-permute-done = f32[32,2,512]{2,1,0:T(2,128)S(1)} collective-permute-done((f32[32,2,512]{2,1,0:T(2,128)S(1)}, f32[32,2,512]{2,1,0:T(2,128)S(1)}, u32[]{:S(2)}, u32[]{:S(2)}) %collective-permute-start) | collective-permute-done | bytes 131104 | tf_op jit(solution)/shard_map/while/body/eval_jaxpr/ppermute | solution.py:11
  304.0 10.9 %collective-permute-done = f32[32,2,512]{2,1,0:T(2,128)S(1)} collective-permute-done((f32[32,2,512]{2,1,0:T(2,128)S(1)}, f32[32,2,512]{2,1,0:T(2,128)S(1)}, u32[]{:S(2)}, u32[]{:S(2)}) %collective-permute-start) | collective-permute-done | bytes 131104 | tf_op jit(solution)/shard_map/while/body/eval_jaxpr/ppermute | solution.py:11
  317.8 10.9 %collective-permute-done = f32[32,2,512]{2,1,0:T(2,128)S(1)} collective-permute-done((f32[32,2,512]{2,1,0:T(2,128)S(1)}, f32[32,2,512]{2,1,0:T(2,128)S(1)}, u32[]{:S(2)}, u32[]{:S(2)}) %collective-permute-start) | collective-permute-done | bytes 131104 | tf_op jit(solution)/shard_map/while/body/eval_jaxpr/ppermute | solution.py:11
  331.7 10.9 %collective-permute-done = f32[32,2,512]{2,1,0:T(2,128)S(1)} collective-permute-done((f32[32,2,512]{2,1,0:T(2,128)S(1)}, f32[32,2,512]{2,1,0:T(2,128)S(1)}, u32[]{:S(2)}, u32[]{:S(2)}) %collective-permute-start) | collective-permute-done | bytes 131104 | tf_op jit(solution)/shard_map/while/body/eval_jaxpr/ppermute | solution.py:11
  345.6 10.9 %collective-permute-done = f32[32,2,512]{2,1,0:T(2,128)S(1)} collective-permute-done((f32[32,2,512]{2,1,0:T(2,128)S(1)}, f32[32,2,512]{2,1,0:T(2,128)S(1)}, u32[]{:S(2)}, u32[]{:S(2)}) %collective-permute-start) | collective-permute-done | bytes 131104 | tf_op jit(solution)/shard_map/while/body/eval_jaxpr/ppermute | solution.py:11
  (83 shorter events, 86.6 us)
Async XLA Ops:
  2.0 50.5 %all-to-all-start = ((bf16[32,16,2,512]{3,1,2,0:T(8,128)(2,1)}), bf16[32,16,2,512]{3,1,2,0:T(8,128)(2,1)S(1)}, u32[]{:S(2)}, u32[]{:S(2)}) async-start(bf16[32,16,2,512]{3,1,2,0:T(8,128)(2,1)} %stack.16), calls=%async_computation | async-start | bytes 2097152 | tf_op jit(solution)/shard_map/all_to_all | solution.py:39
  22.7 36.0 %copy-start.3 = (bf16[2,512,2,512]{3,2,1,0:T(2,128)(2,1)S(1)}, bf16[2,512,2,512]{3,2,1,0:T(2,128)(2,1)}, u32[]{:S(2)}) copy-start(bf16[2,512,2,512]{3,2,1,0:T(2,128)(2,1)} %param.8) | copy-start | bytes 6291460
  53.6 34.9 %all-to-all-start.1 = ((bf16[32,16,2,512]{3,1,2,0:T(8,128)(2,1)}), bf16[32,16,2,512]{3,1,2,0:T(8,128)(2,1)}, u32[]{:S(2)}, u32[]{:S(2)}) async-start(bf16[32,16,2,512]{3,1,2,0:T(8,128)(2,1)} %stack.18), calls=%async_computation.1 | async-start | bytes 2097152 | tf_op jit(solution)/shard_map/all_to_all | solution.py:39
  60.2 2.5 copy-start.4
  65.0 6.8 %copy-start.8 = (s32[2,512]{1,0:T(2,128)S(1)}, s32[2,512]{1,0:T(2,128)}, u32[]{:S(2)}) copy-start(s32[2,512]{1,0:T(2,128)} %param.11) | copy-start | bytes 12292
  92.3 1.6 copy-start.5
  102.6 4.2 %copy-start = (f32[512,2,512]{0,1,2:T(2,128)S(1)}, f32[512,2,512]{0,1,2:T(2,128)}, u32[]{:S(2)}) copy-start(f32[512,2,512]{0,1,2:T(2,128)} %copy.21) | copy-start | bytes 6291460
  111.0 3.2 copy-start.1
  111.1 3.2 copy-start.2
  129.8 12.9 %collective-permute-start = (f32[32,2,512]{2,1,0:T(2,128)S(1)}, f32[32,2,512]{2,1,0:T(2,128)S(1)}, u32[]{:S(2)}, u32[]{:S(2)}) collective-permute-start(f32[32,2,512]{2,1,0:T(2,128)S(1)} %get-tuple-element.192), channel_id=1, source_target_pairs={{0,32},{32,64},{64,96},{96,128},{128,160},{160,192},{192,224},{224... | collective-permute-start | bytes 393224 | tf_op jit(solution)/shard_map/while/body/eval_jaxpr/ppermute | solution.py:11
  143.7 32.4 %collective-permute-start = (f32[32,2,512]{2,1,0:T(2,128)S(1)}, f32[32,2,512]{2,1,0:T(2,128)S(1)}, u32[]{:S(2)}, u32[]{:S(2)}) collective-permute-start(f32[32,2,512]{2,1,0:T(2,128)S(1)} %get-tuple-element.192), channel_id=1, source_target_pairs={{0,32},{32,64},{64,96},{96,128},{128,160},{160,192},{192,224},{224... | collective-permute-start | bytes 393224 | tf_op jit(solution)/shard_map/while/body/eval_jaxpr/ppermute | solution.py:11
  177.1 12.9 %collective-permute-start = (f32[32,2,512]{2,1,0:T(2,128)S(1)}, f32[32,2,512]{2,1,0:T(2,128)S(1)}, u32[]{:S(2)}, u32[]{:S(2)}) collective-permute-start(f32[32,2,512]{2,1,0:T(2,128)S(1)} %get-tuple-element.192), channel_id=1, source_target_pairs={{0,32},{32,64},{64,96},{96,128},{128,160},{160,192},{192,224},{224... | collective-permute-start | bytes 393224 | tf_op jit(solution)/shard_map/while/body/eval_jaxpr/ppermute | solution.py:11
  191.0 12.9 %collective-permute-start = (f32[32,2,512]{2,1,0:T(2,128)S(1)}, f32[32,2,512]{2,1,0:T(2,128)S(1)}, u32[]{:S(2)}, u32[]{:S(2)}) collective-permute-start(f32[32,2,512]{2,1,0:T(2,128)S(1)} %get-tuple-element.192), channel_id=1, source_target_pairs={{0,32},{32,64},{64,96},{96,128},{128,160},{160,192},{192,224},{224... | collective-permute-start | bytes 393224 | tf_op jit(solution)/shard_map/while/body/eval_jaxpr/ppermute | solution.py:11
  204.9 12.9 %collective-permute-start = (f32[32,2,512]{2,1,0:T(2,128)S(1)}, f32[32,2,512]{2,1,0:T(2,128)S(1)}, u32[]{:S(2)}, u32[]{:S(2)}) collective-permute-start(f32[32,2,512]{2,1,0:T(2,128)S(1)} %get-tuple-element.192), channel_id=1, source_target_pairs={{0,32},{32,64},{64,96},{96,128},{128,160},{160,192},{192,224},{224... | collective-permute-start | bytes 393224 | tf_op jit(solution)/shard_map/while/body/eval_jaxpr/ppermute | solution.py:11
  218.7 12.9 %collective-permute-start = (f32[32,2,512]{2,1,0:T(2,128)S(1)}, f32[32,2,512]{2,1,0:T(2,128)S(1)}, u32[]{:S(2)}, u32[]{:S(2)}) collective-permute-start(f32[32,2,512]{2,1,0:T(2,128)S(1)} %get-tuple-element.192), channel_id=1, source_target_pairs={{0,32},{32,64},{64,96},{96,128},{128,160},{160,192},{192,224},{224... | collective-permute-start | bytes 393224 | tf_op jit(solution)/shard_map/while/body/eval_jaxpr/ppermute | solution.py:11
  232.6 12.9 %collective-permute-start = (f32[32,2,512]{2,1,0:T(2,128)S(1)}, f32[32,2,512]{2,1,0:T(2,128)S(1)}, u32[]{:S(2)}, u32[]{:S(2)}) collective-permute-start(f32[32,2,512]{2,1,0:T(2,128)S(1)} %get-tuple-element.192), channel_id=1, source_target_pairs={{0,32},{32,64},{64,96},{96,128},{128,160},{160,192},{192,224},{224... | collective-permute-start | bytes 393224 | tf_op jit(solution)/shard_map/while/body/eval_jaxpr/ppermute | solution.py:11
  246.5 12.9 %collective-permute-start = (f32[32,2,512]{2,1,0:T(2,128)S(1)}, f32[32,2,512]{2,1,0:T(2,128)S(1)}, u32[]{:S(2)}, u32[]{:S(2)}) collective-permute-start(f32[32,2,512]{2,1,0:T(2,128)S(1)} %get-tuple-element.192), channel_id=1, source_target_pairs={{0,32},{32,64},{64,96},{96,128},{128,160},{160,192},{192,224},{224... | collective-permute-start | bytes 393224 | tf_op jit(solution)/shard_map/while/body/eval_jaxpr/ppermute | solution.py:11
  260.4 12.9 %collective-permute-start = (f32[32,2,512]{2,1,0:T(2,128)S(1)}, f32[32,2,512]{2,1,0:T(2,128)S(1)}, u32[]{:S(2)}, u32[]{:S(2)}) collective-permute-start(f32[32,2,512]{2,1,0:T(2,128)S(1)} %get-tuple-element.192), channel_id=1, source_target_pairs={{0,32},{32,64},{64,96},{96,128},{128,160},{160,192},{192,224},{224... | collective-permute-start | bytes 393224 | tf_op jit(solution)/shard_map/while/body/eval_jaxpr/ppermute | solution.py:11
  274.2 12.9 %collective-permute-start = (f32[32,2,512]{2,1,0:T(2,128)S(1)}, f32[32,2,512]{2,1,0:T(2,128)S(1)}, u32[]{:S(2)}, u32[]{:S(2)}) collective-permute-start(f32[32,2,512]{2,1,0:T(2,128)S(1)} %get-tuple-element.192), channel_id=1, source_target_pairs={{0,32},{32,64},{64,96},{96,128},{128,160},{160,192},{192,224},{224... | collective-permute-start | bytes 393224 | tf_op jit(solution)/shard_map/while/body/eval_jaxpr/ppermute | solution.py:11
  288.1 12.9 %collective-permute-start = (f32[32,2,512]{2,1,0:T(2,128)S(1)}, f32[32,2,512]{2,1,0:T(2,128)S(1)}, u32[]{:S(2)}, u32[]{:S(2)}) collective-permute-start(f32[32,2,512]{2,1,0:T(2,128)S(1)} %get-tuple-element.192), channel_id=1, source_target_pairs={{0,32},{32,64},{64,96},{96,128},{128,160},{160,192},{192,224},{224... | collective-permute-start | bytes 393224 | tf_op jit(solution)/shard_map/while/body/eval_jaxpr/ppermute | solution.py:11
  302.0 12.9 %collective-permute-start = (f32[32,2,512]{2,1,0:T(2,128)S(1)}, f32[32,2,512]{2,1,0:T(2,128)S(1)}, u32[]{:S(2)}, u32[]{:S(2)}) collective-permute-start(f32[32,2,512]{2,1,0:T(2,128)S(1)} %get-tuple-element.192), channel_id=1, source_target_pairs={{0,32},{32,64},{64,96},{96,128},{128,160},{160,192},{192,224},{224... | collective-permute-start | bytes 393224 | tf_op jit(solution)/shard_map/while/body/eval_jaxpr/ppermute | solution.py:11
  315.9 12.9 %collective-permute-start = (f32[32,2,512]{2,1,0:T(2,128)S(1)}, f32[32,2,512]{2,1,0:T(2,128)S(1)}, u32[]{:S(2)}, u32[]{:S(2)}) collective-permute-start(f32[32,2,512]{2,1,0:T(2,128)S(1)} %get-tuple-element.192), channel_id=1, source_target_pairs={{0,32},{32,64},{64,96},{96,128},{128,160},{160,192},{192,224},{224... | collective-permute-start | bytes 393224 | tf_op jit(solution)/shard_map/while/body/eval_jaxpr/ppermute | solution.py:11
  329.8 12.9 %collective-permute-start = (f32[32,2,512]{2,1,0:T(2,128)S(1)}, f32[32,2,512]{2,1,0:T(2,128)S(1)}, u32[]{:S(2)}, u32[]{:S(2)}) collective-permute-start(f32[32,2,512]{2,1,0:T(2,128)S(1)} %get-tuple-element.192), channel_id=1, source_target_pairs={{0,32},{32,64},{64,96},{96,128},{128,160},{160,192},{192,224},{224... | collective-permute-start | bytes 393224 | tf_op jit(solution)/shard_map/while/body/eval_jaxpr/ppermute | solution.py:11
  343.6 12.9 %collective-permute-start = (f32[32,2,512]{2,1,0:T(2,128)S(1)}, f32[32,2,512]{2,1,0:T(2,128)S(1)}, u32[]{:S(2)}, u32[]{:S(2)}) collective-permute-start(f32[32,2,512]{2,1,0:T(2,128)S(1)} %get-tuple-element.192), channel_id=1, source_target_pairs={{0,32},{32,64},{64,96},{96,128},{128,160},{160,192},{192,224},{224... | collective-permute-start | bytes 393224 | tf_op jit(solution)/shard_map/while/body/eval_jaxpr/ppermute | solution.py:11
  (2 other events, 1.9 us)
